TPU v7x, 512 devices: a whole 4x8x8 slice. The times are simulated.
512 devices in a mesh: ctx: 64 (over y, x, core), head: 8 (over z).
Axes of the slice: x: 4, y: 8, z: 8, core: 2. Of those that a mesh axis runs over, the one named last changes fastest.
Arguments:
- tokens: bfloat16 [65536, 2048], P('ctx', 'head'), may hold values from -6 to 6
- w_qkv: bfloat16 [3, 2048, 2048], P(None, 'ctx', 'head'), may hold values from -0.125 to 0.125
- out_gain: float32 [2048], P('head'), may hold values from 0.25 to 1.75
- seg_ids: int32 [65536], P('ctx'), may hold values from 0 to 15, never falling along the last dimension, each value on 1 to 16384 neighbouring positions
Outputs:
- attended: bfloat16 [65536, 2048], P('ctx', 'head')
Inputs may be any that keep to these rules, and one draw needn't show every extreme that they name: `seg_ids`: segment numbers never fall along the stream; each segment covers 1 to 16384 consecutive tokens, and one covers exactly 16384.
All inputs are finite; a program needn't handle non-finite values.
Results may differ from a plain program's by a relative error of at most 0.012.
Values may be sent and summed in bfloat16 or wider, within the bound.
No kernel may reach another device: no remote copies, remote signals or barrier semaphores. Data moves between devices by JAX's collectives and lax.ppermute only.
A program may use at most 64 MiB of HBM per device.

v0:
```python
import jax
import jax.numpy as jnp
from jax import lax
from jax.sharding import Mesh
from jax.sharding import PartitionSpec as P

HEAD_DIM = 128
SPAN = 16384
CTX = ("y", "x", "core")


def shifted(value, axis, steps, count):
    return lax.ppermute(value, axis, [(source, source + steps) for source in range(count - steps)])


def ring_gather(value, axis, count, dim):
    by_offset = {0: value}
    ahead = value
    behind = value
    for step in range(1, count // 2 + 1):
        ahead = lax.ppermute(ahead, axis, [(j, (j + 1) % count) for j in range(count)])
        by_offset[-step] = ahead
        if step < count - count // 2:
            behind = lax.ppermute(behind, axis, [(j, (j - 1) % count) for j in range(count)])
            by_offset[step] = behind
    low = -(count // 2)
    stacked = jnp.stack([by_offset[off] for off in range(low, low + count)], axis=0)
    ordered = jnp.roll(stacked, lax.axis_index(axis) + low, axis=0)
    moved = jnp.moveaxis(ordered, 0, dim)
    shape = list(value.shape)
    shape[dim] *= count
    return moved.reshape(shape)


def gather_weights(w_local):
    half = w_local.shape[2] // 2
    core = lax.axis_index("core")
    partner = lax.ppermute(w_local, "core", [(0, 1), (1, 0)])
    low_rows = jnp.where(core == 0, w_local[:, :, :half], partner[:, :, half:])
    high_rows = jnp.where(core == 0, partner[:, :, :half], w_local[:, :, half:])
    rows = jnp.concatenate([low_rows, high_rows], axis=1)
    rows = direct_gather(rows, "x", lax.axis_size("x"), 1)
    rows = ring_gather(rows, "y", lax.axis_size("y"), 1)
    other = lax.ppermute(rows, "core", [(0, 1), (1, 0)])
    return jnp.where(
        core == 0, jnp.concatenate([rows, other], axis=2), jnp.concatenate([other, rows], axis=2)
    )


def direct_gather(value, axis, count, dim):
    low = -(count // 2)
    by_offset = {0: value}
    for off in range(low, low + count):
        if off != 0:
            by_offset[off] = lax.ppermute(
                value, axis, [(j, (j - off) % count) for j in range(count)]
            )
    stacked = jnp.stack([by_offset[off] for off in range(low, low + count)], axis=0)
    ordered = jnp.roll(stacked, lax.axis_index(axis) + low, axis=0)
    moved = jnp.moveaxis(ordered, 0, dim)
    shape = list(value.shape)
    shape[dim] *= count
    return moved.reshape(shape)


def feature_map(values):
    return (jax.nn.elu(values.astype(jnp.float32)) + 1.0).astype(jnp.bfloat16)


def state_scan(kv_state, tails, row_count):
    count = lax.axis_size(CTX)
    window = min(count - 1, 1 + (SPAN - 1) // row_count)
    row_len = lax.axis_size("x") * lax.axis_size("core")
    assert window <= 2 * row_len
    me = lax.axis_index(CTX)
    pos = me % row_len
    first = me - pos

    def tail_of(block):
        return jnp.where(block >= 0, tails[jnp.clip(block, 0, count - 1)], -1.0)

    prev_tail = tail_of(me - 1)
    spread = jnp.broadcast_to(kv_state.astype(jnp.bfloat16)[None], (row_len,) + kv_state.shape)
    row = lax.all_to_all(spread, ("x", "core"), 0, 0, tiled=True).astype(jnp.float32)
    places = jnp.arange(row_len)
    row_tails = tail_of(first + places)
    in_last = row_tails == row_tails[row_len - 1]

    def masked(mask):
        return jnp.sum(jnp.where(mask[:, None, None, None], row, 0.0), axis=0)

    y_count = lax.axis_size("y")
    one_back = shifted(masked(in_last).astype(jnp.bfloat16), "y", 1, y_count).astype(jnp.float32)
    two_back = shifted(
        masked(in_last & (places >= pos)).astype(jnp.bfloat16), "y", 2, y_count
    ).astype(jnp.float32)
    state = masked((places < pos) & (row_tails == prev_tail))
    state = state + jnp.where(tail_of(first - 1) == prev_tail, one_back, 0.0)
    if window > row_len:
        state = state + jnp.where(tail_of(first - row_len - 1) == prev_tail, two_back, 0.0)
    return (state, prev_tail)


def per_device(tokens, w_qkv, out_gain, seg_ids):
    whole = lax.all_gather(tokens, "head", axis=1, tiled=True)
    row_count = seg_ids.shape[0]
    groups = lax.axis_size(CTX)
    own_rows = w_qkv.shape[1]
    tail_row = jnp.full((w_qkv.shape[0], 1, w_qkv.shape[2]), seg_ids[-1], w_qkv.dtype)
    carried = gather_weights(jnp.concatenate([w_qkv, tail_row], axis=1))
    carried = carried.reshape(w_qkv.shape[0], groups, own_rows + 1, w_qkv.shape[2])
    w_rows = carried[:, :, :own_rows].reshape(w_qkv.shape[0], groups * own_rows, w_qkv.shape[2])
    tails = carried[0, :, own_rows, 0].astype(jnp.float32)
    key_value = jnp.einsum(
        "tr,grc->gtc", whole, w_rows[1:], preferred_element_type=jnp.float32
    ).astype(jnp.bfloat16)
    head_count = key_value.shape[2] // HEAD_DIM
    key_map = feature_map(key_value[0]).reshape(row_count, head_count, HEAD_DIM)
    values = key_value[1].reshape(row_count, head_count, HEAD_DIM)
    seg_float = seg_ids.astype(jnp.float32)
    tail_id = seg_float[-1]
    key_tail = jnp.where((seg_float == tail_id)[:, None, None], key_map, jnp.zeros_like(key_map))
    kv_state = jnp.einsum("thd,the->hde", key_tail, values, preferred_element_type=jnp.float32)
    tails, kv_state = lax.optimization_barrier((tails, kv_state))
    state_in, tail_in = state_scan(kv_state, tails, row_count)
    query_proj = jnp.einsum("tr,rc->tc", whole, w_rows[0], preferred_element_type=jnp.float32)
    query_proj = lax.reduce_precision(query_proj, exponent_bits=8, mantissa_bits=7)
    queries = feature_map(query_proj).reshape(row_count, head_count, HEAD_DIM)
    block_rows = min(512, row_count)
    pieces = []
    for blk_no in range(row_count // block_rows):
        first_row = blk_no * block_rows
        key_end = first_row + block_rows
        query_blk = queries[first_row:key_end]
        query_pos = first_row + jnp.arange(block_rows, dtype=jnp.int32)
        query_seg = seg_float[first_row:key_end]
        scores = jnp.einsum(
            "bhd,shd->hbs", query_blk, key_map[:key_end], preferred_element_type=jnp.float32
        )
        visible = (jnp.arange(key_end, dtype=jnp.int32)[None, :] <= query_pos[:, None]) & (
            seg_float[None, :key_end] == query_seg[:, None]
        )
        weights = jnp.where(visible[None], scores, 0.0).astype(jnp.bfloat16)
        pieces.append(
            jnp.einsum(
                "hbs,she->bhe", weights, values[:key_end], preferred_element_type=jnp.float32
            )
        )
    local_part = jnp.concatenate(pieces, axis=0)
    state_low = state_in.astype(jnp.bfloat16)
    prefix = jnp.einsum("thd,hde->the", queries, state_low, preferred_element_type=jnp.float32)
    prefix = jnp.where((seg_float == tail_in)[:, None, None], prefix, 0.0)
    numerator = local_part + prefix
    inv_norm = lax.rsqrt(jnp.mean(numerator * numerator, axis=-1, keepdims=True) + 1e-05)
    result = numerator * inv_norm * out_gain.reshape(head_count, HEAD_DIM)
    return result.astype(jnp.bfloat16).reshape(row_count, head_count * HEAD_DIM)


def solution(mesh):
    shape = dict(zip(mesh.axis_names, mesh.devices.shape))
    head = shape["head"]
    fine = Mesh(mesh.devices.reshape(-1, 4, 2, head), (*CTX, "head"))
    placed = (P(CTX, "head"), P(None, CTX, "head"), P("head"), P(CTX))
    return jax.shard_map(
        per_device, mesh=fine, in_specs=placed, out_specs=P(CTX, "head"), check_vma=False
    )
```

profile of v0, /device:TPU:18, one launch (start us, length us, event | category | flops | bytes accessed | tf_op | source)
XLA Modules:
  0.0 132.6 jit_solution(4561768235735514698)
XLA Ops:
  13.9 4.0 %collective-permute-start.1 = (bf16[3,66,128]{2,1,0:T(8,128)(2,1)S(1)}, bf16[3,66,128]{2,1,0:T(8,128)(2,1)S(1)}, u32[]{:S(2)}, u32[]{:S(2)}) collective-permute-start(bf16[3,66,128]{2,1,0:T(8,128)(2,1)S(1)} %pad_maximum_fusion), channel_id=1, source_target_pairs={{0,32},{16,48},{32,0},{48,16},{1,33},{17,49},{33,1},{49,17},{2,34}... | collective-permute-start | bytes 152072 | tf_op jit(solution)/shard_map/ppermute | solution.py:55
  18.0 1.9 %collective-permute-start.2 = (bf16[3,66,128]{2,1,0:T(8,128)(2,1)S(1)}, bf16[3,66,128]{2,1,0:T(8,128)(2,1)S(1)}, u32[]{:S(2)}, u32[]{:S(2)}) collective-permute-start(bf16[3,66,128]{2,1,0:T(8,128)(2,1)S(1)} %pad_maximum_fusion), channel_id=1, source_target_pairs={{0,16},{16,32},{32,48},{48,0},{1,17},{17,33},{33,49},{49,1},{2,18}... | collective-permute-start | bytes 152072 | tf_op jit(solution)/shard_map/ppermute | solution.py:55
  19.9 3.9 %collective-permute-start.3 = (bf16[3,66,128]{2,1,0:T(8,128)(2,1)S(1)}, bf16[3,66,128]{2,1,0:T(8,128)(2,1)S(1)}, u32[]{:S(2)}, u32[]{:S(2)}) collective-permute-start(bf16[3,66,128]{2,1,0:T(8,128)(2,1)S(1)} %pad_maximum_fusion), channel_id=1, source_target_pairs={{0,48},{16,0},{32,16},{48,32},{1,49},{17,1},{33,17},{49,33},{2,50}... | collective-permute-start | bytes 152072 | tf_op jit(solution)/shard_map/ppermute | solution.py:55
  26.2 3.5 %collective-permute-start.4 = (bf16[3,264,128]{2,1,0:T(8,128)(2,1)S(1)}, bf16[3,264,128]{2,1,0:T(8,128)(2,1)S(1)}, u32[]{:S(2)}, u32[]{:S(2)}) collective-permute-start(bf16[3,264,128]{2,1,0:T(8,128)(2,1)S(1)} %reshape.183), channel_id=1, source_target_pairs={{0,64},{64,128},{128,192},{192,256},{256,320},{320,384},{384,448},... | collective-permute-start | bytes 608264 | tf_op jit(solution)/shard_map/ppermute | solution.py:21
  29.7 4.1 %collective-permute-done.4 = bf16[3,264,128]{2,1,0:T(8,128)(2,1)S(1)} collective-permute-done((bf16[3,264,128]{2,1,0:T(8,128)(2,1)S(1)}, bf16[3,264,128]{2,1,0:T(8,128)(2,1)S(1)}, u32[]{:S(2)}, u32[]{:S(2)}) %collective-permute-start.4) | collective-permute-done | bytes 202784 | tf_op jit(solution)/shard_map/ppermute | solution.py:21
  33.9 3.8 %collective-permute-start.5 = (bf16[3,264,128]{2,1,0:T(8,128)(2,1)S(1)}, bf16[3,264,128]{2,1,0:T(8,128)(2,1)S(1)}, u32[]{:S(2)}, u32[]{:S(2)}) collective-permute-start(bf16[3,264,128]{2,1,0:T(8,128)(2,1)S(1)} %collective-permute-done.4), channel_id=1, source_target_pairs={{0,64},{64,128},{128,192},{192,256},{256,320},{320,384},{384,448},... | collective-permute-start | bytes 608264 | tf_op jit(solution)/shard_map/ppermute | solution.py:21
  37.6 4.2 %collective-permute-start.8 = (bf16[3,264,128]{2,1,0:T(8,128)(2,1)S(1)}, bf16[3,264,128]{2,1,0:T(8,128)(2,1)S(1)}, u32[]{:S(2)}, u32[]{:S(2)}) collective-permute-start(bf16[3,264,128]{2,1,0:T(8,128)(2,1)S(1)} %reshape.183), channel_id=1, source_target_pairs={{0,448},{64,0},{128,64},{192,128},{256,192},{320,256},{384,320},{4... | collective-permute-start | bytes 608264 | tf_op jit(solution)/shard_map/ppermute | solution.py:24
  43.6 2.9 %collective-permute-start.6 = (bf16[3,264,128]{2,1,0:T(8,128)(2,1)S(1)}, bf16[3,264,128]{2,1,0:T(8,128)(2,1)S(1)}, u32[]{:S(2)}, u32[]{:S(2)}) collective-permute-start(bf16[3,264,128]{2,1,0:T(8,128)(2,1)S(1)} %collective-permute-done.5), channel_id=1, source_target_pairs={{0,64},{64,128},{128,192},{192,256},{256,320},{320,384},{384,448},... | collective-permute-start | bytes 608264 | tf_op jit(solution)/shard_map/ppermute | solution.py:21
  46.9 3.7 %collective-permute-start.9 = (bf16[3,264,128]{2,1,0:T(8,128)(2,1)S(1)}, bf16[3,264,128]{2,1,0:T(8,128)(2,1)S(1)}, u32[]{:S(2)}, u32[]{:S(2)}) collective-permute-start(bf16[3,264,128]{2,1,0:T(8,128)(2,1)S(1)} %collective-permute-done.8), channel_id=1, source_target_pairs={{0,448},{64,0},{128,64},{192,128},{256,192},{320,256},{384,320},{4... | collective-permute-start | bytes 608264 | tf_op jit(solution)/shard_map/ppermute | solution.py:24
  52.4 2.9 %collective-permute-start.7 = (bf16[3,264,128]{2,1,0:T(8,128)(2,1)S(1)}, bf16[3,264,128]{2,1,0:T(8,128)(2,1)S(1)}, u32[]{:S(2)}, u32[]{:S(2)}) collective-permute-start(bf16[3,264,128]{2,1,0:T(8,128)(2,1)S(1)} %collective-permute-done.6), channel_id=1, source_target_pairs={{0,64},{64,128},{128,192},{192,256},{256,320},{320,384},{384,448},... | collective-permute-start | bytes 608264 | tf_op jit(solution)/shard_map/ppermute | solution.py:21
  55.8 3.8 %collective-permute-start.10 = (bf16[3,264,128]{2,1,0:T(8,128)(2,1)S(1)}, bf16[3,264,128]{2,1,0:T(8,128)(2,1)S(1)}, u32[]{:S(2)}, u32[]{:S(2)}) collective-permute-start(bf16[3,264,128]{2,1,0:T(8,128)(2,1)S(1)} %collective-permute-done.9), channel_id=1, source_target_pairs={{0,448},{64,0},{128,64},{192,128},{256,192},{320,256},{384,320},{4... | collective-permute-start | bytes 608264 | tf_op jit(solution)/shard_map/ppermute | solution.py:24
  61.5 3.2 %collective-permute-done.10 = bf16[3,264,128]{2,1,0:T(8,128)(2,1)S(1)} collective-permute-done((bf16[3,264,128]{2,1,0:T(8,128)(2,1)S(1)}, bf16[3,264,128]{2,1,0:T(8,128)(2,1)S(1)}, u32[]{:S(2)}, u32[]{:S(2)}) %collective-permute-start.10) | collective-permute-done | bytes 202784 | tf_op jit(solution)/shard_map/ppermute | solution.py:24
  66.5 1.9 %collective-permute-start.11 = (bf16[3,2112,128]{2,1,0:T(8,128)(2,1)}, bf16[3,2112,128]{2,1,0:T(8,128)(2,1)}, u32[]{:S(2)}, u32[]{:S(2)}) collective-permute-start(bf16[3,2112,128]{2,1,0:T(8,128)(2,1)} %bitcast.14), channel_id=1, source_target_pairs={{0,8},{8,0},{1,9},{9,1},{2,10},{10,2},{3,11},{11,3},{4,12},{12,4},... | collective-permute-start | bytes 4866056 | tf_op jit(solution)/shard_map/ppermute | solution.py:44
  72.1 2.5 %concatenate.35 = bf16[3,64,33,128]{3,2,1,0:T(8,128)(2,1)S(1)} reshape(bf16[3,8,264,128]{3,2,1,0:T(8,128)(2,1)} %copy.31) | data formatting | bytes 3244032 | tf_op jit(solution)/shard_map/concatenate | solution.py:46
  74.5 3.7 %concatenate.36 = bf16[3,64,33,128]{3,2,1,0:T(8,128)(2,1)} reshape(bf16[3,2112,128]{2,1,0:T(8,128)(2,1)} %collective-permute-done.11) | data formatting | bytes 3244032 | tf_op jit(solution)/shard_map/concatenate | solution.py:46
  78.2 2.8 %maximum_select_fusion = bf16[3,64,33,256]{3,2,1,0:T(8,128)(2,1)S(1)} fusion(bf16[3,64,33,128]{3,2,1,0:T(8,128)(2,1)} %concatenate.36, bf16[3,64,33,128]{3,2,1,0:T(8,128)(2,1)S(1)} %concatenate.35, pred[]{:T(512)S(6)} %eq.87), kind=kLoop, calls=%fused_computation.4 | loop fusion | flops 14598144 | bytes 6488065 | tf_op jit(solution)/shard_map/jit(_where)/select_n | solution.py:45
  83.0 4.1 %all-gather.2.cloned.1.call-done = bf16[1024,2048]{1,0:T(8,128)(2,1)} async-done(((bf16[1024,256]{1,0:T(8,128)(2,1)}), bf16[1024,2048]{1,0:T(8,128)(2,1)}) %all-gather.2.cloned.1.call-update) | async-done | bytes 4194320 | tf_op jit(solution)/shard_map/all_gather | solution.py:105
  87.2 4.6 %fusion.7 = bf16[2,1024,256]{1,2,0:T(8,128)(2,1)S(1)} fusion(bf16[2,2048,256]{2,1,0:T(8,128)(2,1)S(1)} %bitcast.97, bf16[1024,2048]{1,0:T(8,128)(2,1)} %all-gather.2.cloned.1.call-done), kind=kOutput, calls=%fused_computation.20 | convolution fusion | flops 2148007936 | bytes 7340032 | tf_op jit(solution)/shard_map/tr,grc->gtc/dot_general | solution.py:114
  94.3 4.8 %all-to-all-start = ((bf16[8,2,128,128]{3,2,1,0:T(8,128)(2,1)}), bf16[8,2,128,128]{3,2,1,0:T(8,128)(2,1)S(1)}, u32[]{:S(2)}, u32[]{:S(2)}) async-start(bf16[8,2,128,128]{3,2,1,0:T(8,128)(2,1)} %broadcast_in_dim.115), calls=%async_computation | async-start | bytes 1048576 | tf_op jit(solution)/shard_map/all_to_all | solution.py:84
  101.6 4.2 %fusion.21 = bf16[1024,256]{0,1:T(8,128)(2,1)S(1)} fusion(bf16[2048,256]{1,0:T(8,128)(2,1)} %bitcast.101, bf16[1024,2048]{1,0:T(8,128)(2,1)} %all-gather.2.cloned.1.call-done), kind=kOutput, calls=%fused_computation.34 | convolution fusion | flops 1075314688 | bytes 5767168 | tf_op jit(solution)/shard_map/tr,rc->tc/dot_general | solution.py:126
  109.3 2.8 %fusion.14 = f32[512,2,128]{0,2,1:T(8,128)S(1)} fusion(bf16[1024,2,128]{0,2,1:T(8,128)(2,1)} %bitcast.103, bf16[512,2,128]{0,2,1:T(8,128)(2,1)} %bitcast.106, pred[512,1024]{1,0:T(8,128)(4,1)} %fusion.2, f32[1024,2,128]{0,2,1:T(8,128)S(1)} %bitcast.100), kind=kOutput, calls=%fused_computation.27 | convolution fusion | flops 540278784 | bytes 2883584 | tf_op jit(solution)/shard_map/hbs,she->bhe/dot_general | solution.py:145
  112.5 5.5 %collective-permute-start.13 = (bf16[2,128,128]{2,1,0:T(8,128)(2,1)S(1)}, bf16[2,128,128]{2,1,0:T(8,128)(2,1)S(1)}, u32[]{:S(2)}, u32[]{:S(2)}) collective-permute-start(bf16[2,128,128]{2,1,0:T(8,128)(2,1)S(1)} %get-tuple-element.10), channel_id=1, source_target_pairs={{0,128},{64,192},{128,256},{192,320},{256,384},{320,448},{1,129},{... | collective-permute-start | bytes 196616 | tf_op jit(solution)/shard_map/ppermute | solution.py:13
  118.0 2.5 %collective-permute-start.12 = (bf16[2,128,128]{2,1,0:T(8,128)(2,1)S(1)}, bf16[2,128,128]{2,1,0:T(8,128)(2,1)S(1)}, u32[]{:S(2)}, u32[]{:S(2)}) collective-permute-start(bf16[2,128,128]{2,1,0:T(8,128)(2,1)S(1)} %get-tuple-element.9), channel_id=1, source_target_pairs={{0,64},{64,128},{128,192},{192,256},{256,320},{320,384},{384,448},... | collective-permute-start | bytes 196616 | tf_op jit(solution)/shard_map/ppermute | solution.py:13
  121.8 2.4 %collective-permute-done.12 = bf16[2,128,128]{2,1,0:T(8,128)(2,1)S(1)} collective-permute-done((bf16[2,128,128]{2,1,0:T(8,128)(2,1)S(1)}, bf16[2,128,128]{2,1,0:T(8,128)(2,1)S(1)}, u32[]{:S(2)}, u32[]{:S(2)}) %collective-permute-start.12) | collective-permute-done | bytes 65568 | tf_op jit(solution)/shard_map/ppermute | solution.py:13
  (85 shorter events, 33.0 us)
Async XLA Ops:
  6.5 80.7 %all-gather.2.cloned.1.call-start = ((), (), s32[]{:S(2)}) async-start(), calls=%async_computation.1 | async-start | bytes 4718592 | tf_op jit(solution)/shard_map/all_gather | solution.py:105
  9.3 3.1 %collective-permute-start = (bf16[3,33,256]{2,1,0:T(8,128)(2,1)S(1)}, bf16[3,33,256]{2,1,0:T(8,128)(2,1)S(1)}, u32[]{:S(2)}, u32[]{:S(2)}) collective-permute-start(bf16[3,33,256]{2,1,0:T(8,128)(2,1)S(1)} %concatenate.31), channel_id=1, source_target_pairs={{0,8},{8,0},{1,9},{9,1},{2,10},{10,2},{3,11},{11,3},{4,12},{12,4},... | collective-permute-start | bytes 152072 | tf_op jit(solution)/shard_map/ppermute | solution.py:38
  13.9 10.0 %collective-permute-start.1 = (bf16[3,66,128]{2,1,0:T(8,128)(2,1)S(1)}, bf16[3,66,128]{2,1,0:T(8,128)(2,1)S(1)}, u32[]{:S(2)}, u32[]{:S(2)}) collective-permute-start(bf16[3,66,128]{2,1,0:T(8,128)(2,1)S(1)} %pad_maximum_fusion), channel_id=1, source_target_pairs={{0,32},{16,48},{32,0},{48,16},{1,33},{17,49},{33,1},{49,17},{2,34}... | collective-permute-start | bytes 152072 | tf_op jit(solution)/shard_map/ppermute | solution.py:55
  18.0 6.0 %collective-permute-start.2 = (bf16[3,66,128]{2,1,0:T(8,128)(2,1)S(1)}, bf16[3,66,128]{2,1,0:T(8,128)(2,1)S(1)}, u32[]{:S(2)}, u32[]{:S(2)}) collective-permute-start(bf16[3,66,128]{2,1,0:T(8,128)(2,1)S(1)} %pad_maximum_fusion), channel_id=1, source_target_pairs={{0,16},{16,32},{32,48},{48,0},{1,17},{17,33},{33,49},{49,1},{2,18}... | collective-permute-start | bytes 152072 | tf_op jit(solution)/shard_map/ppermute | solution.py:55
  19.9 6.0 %collective-permute-start.3 = (bf16[3,66,128]{2,1,0:T(8,128)(2,1)S(1)}, bf16[3,66,128]{2,1,0:T(8,128)(2,1)S(1)}, u32[]{:S(2)}, u32[]{:S(2)}) collective-permute-start(bf16[3,66,128]{2,1,0:T(8,128)(2,1)S(1)} %pad_maximum_fusion), channel_id=1, source_target_pairs={{0,48},{16,0},{32,16},{48,32},{1,49},{17,1},{33,17},{49,33},{2,50}... | collective-permute-start | bytes 152072 | tf_op jit(solution)/shard_map/ppermute | solution.py:55
  26.2 7.6 %collective-permute-start.4 = (bf16[3,264,128]{2,1,0:T(8,128)(2,1)S(1)}, bf16[3,264,128]{2,1,0:T(8,128)(2,1)S(1)}, u32[]{:S(2)}, u32[]{:S(2)}) collective-permute-start(bf16[3,264,128]{2,1,0:T(8,128)(2,1)S(1)} %reshape.183), channel_id=1, source_target_pairs={{0,64},{64,128},{128,192},{192,256},{256,320},{320,384},{384,448},... | collective-permute-start | bytes 608264 | tf_op jit(solution)/shard_map/ppermute | solution.py:21
  33.9 9.7 %collective-permute-start.5 = (bf16[3,264,128]{2,1,0:T(8,128)(2,1)S(1)}, bf16[3,264,128]{2,1,0:T(8,128)(2,1)S(1)}, u32[]{:S(2)}, u32[]{:S(2)}) collective-permute-start(bf16[3,264,128]{2,1,0:T(8,128)(2,1)S(1)} %collective-permute-done.4), channel_id=1, source_target_pairs={{0,64},{64,128},{128,192},{192,256},{256,320},{320,384},{384,448},... | collective-permute-start | bytes 608264 | tf_op jit(solution)/shard_map/ppermute | solution.py:21
  37.6 9.3 %collective-permute-start.8 = (bf16[3,264,128]{2,1,0:T(8,128)(2,1)S(1)}, bf16[3,264,128]{2,1,0:T(8,128)(2,1)S(1)}, u32[]{:S(2)}, u32[]{:S(2)}) collective-permute-start(bf16[3,264,128]{2,1,0:T(8,128)(2,1)S(1)} %reshape.183), channel_id=1, source_target_pairs={{0,448},{64,0},{128,64},{192,128},{256,192},{320,256},{384,320},{4... | collective-permute-start | bytes 608264 | tf_op jit(solution)/shard_map/ppermute | solution.py:24
  43.6 8.8 %collective-permute-start.6 = (bf16[3,264,128]{2,1,0:T(8,128)(2,1)S(1)}, bf16[3,264,128]{2,1,0:T(8,128)(2,1)S(1)}, u32[]{:S(2)}, u32[]{:S(2)}) collective-permute-start(bf16[3,264,128]{2,1,0:T(8,128)(2,1)S(1)} %collective-permute-done.5), channel_id=1, source_target_pairs={{0,64},{64,128},{128,192},{192,256},{256,320},{320,384},{384,448},... | collective-permute-start | bytes 608264 | tf_op jit(solution)/shard_map/ppermute | solution.py:21
  46.9 8.8 %collective-permute-start.9 = (bf16[3,264,128]{2,1,0:T(8,128)(2,1)S(1)}, bf16[3,264,128]{2,1,0:T(8,128)(2,1)S(1)}, u32[]{:S(2)}, u32[]{:S(2)}) collective-permute-start(bf16[3,264,128]{2,1,0:T(8,128)(2,1)S(1)} %collective-permute-done.8), channel_id=1, source_target_pairs={{0,448},{64,0},{128,64},{192,128},{256,192},{320,256},{384,320},{4... | collective-permute-start | bytes 608264 | tf_op jit(solution)/shard_map/ppermute | solution.py:24
  52.4 8.8 %collective-permute-start.7 = (bf16[3,264,128]{2,1,0:T(8,128)(2,1)S(1)}, bf16[3,264,128]{2,1,0:T(8,128)(2,1)S(1)}, u32[]{:S(2)}, u32[]{:S(2)}) collective-permute-start(bf16[3,264,128]{2,1,0:T(8,128)(2,1)S(1)} %collective-permute-done.6), channel_id=1, source_target_pairs={{0,64},{64,128},{128,192},{192,256},{256,320},{320,384},{384,448},... | collective-permute-start | bytes 608264 | tf_op jit(solution)/shard_map/ppermute | solution.py:21
  55.8 8.9 %collective-permute-start.10 = (bf16[3,264,128]{2,1,0:T(8,128)(2,1)S(1)}, bf16[3,264,128]{2,1,0:T(8,128)(2,1)S(1)}, u32[]{:S(2)}, u32[]{:S(2)}) collective-permute-start(bf16[3,264,128]{2,1,0:T(8,128)(2,1)S(1)} %collective-permute-done.9), channel_id=1, source_target_pairs={{0,448},{64,0},{128,64},{192,128},{256,192},{320,256},{384,320},{4... | collective-permute-start | bytes 608264 | tf_op jit(solution)/shard_map/ppermute | solution.py:24
  65.0 4.0 %copy-start.1 = (s32[1024]{0:T(1024)S(1)}, s32[1024]{0:T(1024)}, u32[]{:S(2)}) copy-start(s32[1024]{0:T(1024)} %param.7) | copy-start | bytes 12292
  66.5 8.0 %collective-permute-start.11 = (bf16[3,2112,128]{2,1,0:T(8,128)(2,1)}, bf16[3,2112,128]{2,1,0:T(8,128)(2,1)}, u32[]{:S(2)}, u32[]{:S(2)}) collective-permute-start(bf16[3,2112,128]{2,1,0:T(8,128)(2,1)} %bitcast.14), channel_id=1, source_target_pairs={{0,8},{8,0},{1,9},{9,1},{2,10},{10,2},{3,11},{11,3},{4,12},{12,4},... | collective-permute-start | bytes 4866056 | tf_op jit(solution)/shard_map/ppermute | solution.py:44
  92.0 2.3 %copy-start = (bf16[1,1024,256]{1,2,0:T(8,128)(2,1)}, bf16[1,1024,256]{1,2,0:T(8,128)(2,1)S(1)}, u32[]{:S(2)}) copy-start(bf16[1,1024,256]{1,2,0:T(8,128)(2,1)S(1)} %get-tuple-element.17) | copy-start | bytes 1572868
  94.3 17.9 %all-to-all-start = ((bf16[8,2,128,128]{3,2,1,0:T(8,128)(2,1)}), bf16[8,2,128,128]{3,2,1,0:T(8,128)(2,1)S(1)}, u32[]{:S(2)}, u32[]{:S(2)}) async-start(bf16[8,2,128,128]{3,2,1,0:T(8,128)(2,1)} %broadcast_in_dim.115), calls=%async_computation | async-start | bytes 1048576 | tf_op jit(solution)/shard_map/all_to_all | solution.py:84
  112.2 12.4 %copy-start.2 = (f32[256]{0:T(256)S(1)}, f32[256]{0:T(256)}, u32[]{:S(2)}) copy-start(f32[256]{0:T(256)} %param.6) | copy-start | bytes 3076
  112.5 9.3 %collective-permute-start.13 = (bf16[2,128,128]{2,1,0:T(8,128)(2,1)S(1)}, bf16[2,128,128]{2,1,0:T(8,128)(2,1)S(1)}, u32[]{:S(2)}, u32[]{:S(2)}) collective-permute-start(bf16[2,128,128]{2,1,0:T(8,128)(2,1)S(1)} %get-tuple-element.10), channel_id=1, source_target_pairs={{0,128},{64,192},{128,256},{192,320},{256,384},{320,448},{1,129},{... | collective-permute-start | bytes 196616 | tf_op jit(solution)/shard_map/ppermute | solution.py:13
  118.0 6.2 %collective-permute-start.12 = (bf16[2,128,128]{2,1,0:T(8,128)(2,1)S(1)}, bf16[2,128,128]{2,1,0:T(8,128)(2,1)S(1)}, u32[]{:S(2)}, u32[]{:S(2)}) collective-permute-start(bf16[2,128,128]{2,1,0:T(8,128)(2,1)S(1)} %get-tuple-element.9), channel_id=1, source_target_pairs={{0,64},{64,128},{128,192},{192,256},{256,320},{320,384},{384,448},... | collective-permute-start | bytes 196616 | tf_op jit(solution)/shard_map/ppermute | solution.py:13
Sparse Core Ops, SparseCore 0:
  18.1 69.0 all-gather.1
where the time goes:
time: 134 us; the launch traced here: 133 us
  starting transfers between devices  51.1 us (38%)
  waiting for transfers between devices  23.2 us (17%)
  local copies, waits for them, and re-layouts  17.8 us (13%)
  between operations  15.9 us (12%)
  matrix products  14.4 us (11%)
  other arithmetic  10.1 us (8%)
    ppermute x4, starting transfers between devices, ring_gather(): lax.ppermute(ahead, axis, [(j, (j + 1) % count) for j in range(count)])  13 us
    ppermute x3, starting transfers between devices, ring_gather(): lax.ppermute(behind, axis, [(j, (j - 1) % count) for j in range(count)])  11.6 us
    ppermute x3, starting transfers between devices, direct_gather(): lax.ppermute(value, axis, [(j, (j - off) % count) for j in range(count)])  9.88 us
    ppermute x4, waiting for transfers between devices, ring_gather(): lax.ppermute(ahead, axis, [(j, (j + 1) % count) for j in range(count)])  9.33 us
    ppermute x2, starting transfers between devices, shifted(): lax.ppermute(value, axis, [(source, source + steps) for source in range(c...  8.02 us
    concatenate x2, local copies, waits for them, and re-layouts, gather_weights(): jnp.concatenate([rows, other], axis=2)  6.16 us
    all_to_all x1, starting transfers between devices, state_scan(): lax.all_to_all(spread, ('x', 'core'), 0, 0, tiled=True).astype(jnp.float32)  4.78 us
    dot_general x2, matrix products, per_device(): jnp.einsum('hbs,she->bhe', weights, values[:key_end], preferred_element_t...  4.73 us
  transfers between devices with their start and end apart: 16, of which 12 were waited for; matrix products, arithmetic and copies ran while one was open for 22% of the time, Pallas kernels for 0%

commit v1 on v0

--- a/solution.py
+++ b/solution.py
@@ -7,6 +7,13 @@
 HEAD_DIM = 128
 SPAN = 16384
 CTX = ("y", "x", "core")
+
+
+def swapped_in(x, axis, dim):
+    n_dev = lax.axis_size(axis)
+    pieces = jnp.stack([x for _ in range(n_dev)])
+    pieces = lax.all_to_all(pieces, axis, split_axis=0, concat_axis=0)
+    return jnp.concatenate(pieces, axis=dim)
 
 
 def shifted(value, axis, steps, count):
@@ -102,7 +109,7 @@
 
 
 def per_device(tokens, w_qkv, out_gain, seg_ids):
-    whole = lax.all_gather(tokens, "head", axis=1, tiled=True)
+    whole = swapped_in(tokens, "head", 1)
     row_count = seg_ids.shape[0]
     groups = lax.axis_size(CTX)
     own_rows = w_qkv.shape[1]

time: 134 us -> 180 us (1.34)
  waiting for transfers between devices: 23.2 us -> 51.1 us
  local copies, waits for them, and re-layouts: 17.8 us -> 39.8 us
  between operations: 15.9 us -> 2.55 us
  starting transfers between devices: 51.1 us -> 60.8 us
    all_to_all x0 -> x1, waiting for transfers between devices: none -> 31.1 us  [swapped_in(): pieces = lax.all_to_all(pieces, axis, split_axis=0, concat_axis=0)]
    reshape x0 -> x3, local copies, waits for them, and re-layouts: none -> 18.7 us  [swapped_in(): return jnp.concatenate(pieces, axis=dim)]
    all_to_all x0 -> x1, starting transfers between devices: none -> 10.3 us  [swapped_in(): pieces = lax.all_to_all(pieces, axis, split_axis=0, concat_axis=0)]
    ppermute x3, starting transfers between devices: 11.6 us -> 5.87 us  [ring_gather(): lax.ppermute(behind, axis, [(j, (j - 1) % count) for j in range(count)])]
    ppermute x4, starting transfers between devices: 13 us -> 17.8 us  [ring_gather(): lax.ppermute(ahead, axis, [(j, (j + 1) % count) for j in range(count)])]
    all_gather x1 -> x0, waiting for transfers between devices: 4.14 us -> none  [per_device(): whole = lax.all_gather(tokens, 'head', axis=1, tiled=True)]
    another operation x0 -> x1, local copies, waits for them, and re-layouts: none -> 3.29 us  [swapped_in(): pieces = jnp.stack([x for _ in range(n_dev)])]
    ppermute x3, waiting for transfers between devices: 4.11 us -> 6.81 us  [ring_gather(): lax.ppermute(behind, axis, [(j, (j - 1) % count) for j in range(count)])]
  transfers between devices with their start and end apart: 16 -> 16, of which waited for: 12 -> 12; matrix products, arithmetic and copies ran while one was open for 22% -> 18% of each run, Pallas kernels for 0% -> 0%
where the time goes in v1:
time: 180 us; the launch traced here: 179 us
  starting transfers between devices  60.8 us (34%)
  waiting for transfers between devices  51.1 us (28%)
  local copies, waits for them, and re-layouts  39.8 us (22%)
  matrix products  14.5 us (8%)
  other arithmetic  10.2 us (6%)
  between operations  2.55 us (1%)
    all_to_all x1, waiting for transfers between devices, swapped_in(): pieces = lax.all_to_all(pieces, axis, split_axis=0, concat_axis=0)  31.1 us
    reshape x3, local copies, waits for them, and re-layouts, swapped_in(): return jnp.concatenate(pieces, axis=dim)  18.7 us
    ppermute x4, starting transfers between devices, ring_gather(): lax.ppermute(ahead, axis, [(j, (j + 1) % count) for j in range(count)])  17.8 us
    all_to_all x1, starting transfers between devices, swapped_in(): pieces = lax.all_to_all(pieces, axis, split_axis=0, concat_axis=0)  10.3 us
    ppermute x3, starting transfers between devices, direct_gather(): lax.ppermute(value, axis, [(j, (j - off) % count) for j in range(count)])  9.86 us
    ppermute x2, starting transfers between devices, shifted(): lax.ppermute(value, axis, [(source, source + steps) for source in range(c...  8.3 us
    ppermute x4, waiting for transfers between devices, ring_gather(): lax.ppermute(ahead, axis, [(j, (j + 1) % count) for j in range(count)])  7.62 us
    ppermute x3, waiting for transfers between devices, ring_gather(): lax.ppermute(behind, axis, [(j, (j - 1) % count) for j in range(count)])  6.81 us
  transfers between devices with their start and end apart: 16, of which 12 were waited for; matrix products, arithmetic and copies ran while one was open for 18% of the time, Pallas kernels for 0%

profile of v1, /device:TPU:18, one launch (start us, length us, event | category | flops | bytes accessed | tf_op | source)
XLA Modules:
  0.0 178.9 jit_solution(15855963912923644055)
XLA Ops:
  7.4 4.0 %collective-permute-start.1 = (bf16[3,66,128]{2,1,0:T(8,128)(2,1)S(1)}, bf16[3,66,128]{2,1,0:T(8,128)(2,1)S(1)}, u32[]{:S(2)}, u32[]{:S(2)}) collective-permute-start(bf16[3,66,128]{2,1,0:T(8,128)(2,1)S(1)} %pad_maximum_fusion), channel_id=1, source_target_pairs={{0,32},{16,48},{32,0},{48,16},{1,33},{17,49},{33,1},{49,17},{2,34}... | collective-permute-start | bytes 152072 | tf_op jit(solution)/shard_map/ppermute | solution.py:62
  11.4 3.3 %stack.57 = bf16[8,1024,256]{2,1,0:T(8,128)(2,1)} broadcast(bf16[1024,256]{1,0:T(8,128)(2,1)} %param.4), dimensions={1,2} | broadcast | bytes 4718592 | tf_op jit(solution)/shard_map/stack | solution.py:14
  14.7 10.3 %all-to-all-start = ((bf16[8,1024,256]{2,1,0:T(8,128)(2,1)}), bf16[8,1024,256]{2,1,0:T(8,128)(2,1)}, u32[]{:S(2)}, u32[]{:S(2)}) async-start(bf16[8,1024,256]{2,1,0:T(8,128)(2,1)} %stack.57), calls=%async_computation | async-start | bytes 8388608 | tf_op jit(solution)/shard_map/all_to_all | solution.py:15
  27.0 3.9 %collective-permute-start.3 = (bf16[3,66,128]{2,1,0:T(8,128)(2,1)S(1)}, bf16[3,66,128]{2,1,0:T(8,128)(2,1)S(1)}, u32[]{:S(2)}, u32[]{:S(2)}) collective-permute-start(bf16[3,66,128]{2,1,0:T(8,128)(2,1)S(1)} %pad_maximum_fusion), channel_id=1, source_target_pairs={{0,48},{16,0},{32,16},{48,32},{1,49},{17,1},{33,17},{49,33},{2,50}... | collective-permute-start | bytes 152072 | tf_op jit(solution)/shard_map/ppermute | solution.py:62
  33.2 3.5 %collective-permute-start.4 = (bf16[3,264,128]{2,1,0:T(8,128)(2,1)S(1)}, bf16[3,264,128]{2,1,0:T(8,128)(2,1)S(1)}, u32[]{:S(2)}, u32[]{:S(2)}) collective-permute-start(bf16[3,264,128]{2,1,0:T(8,128)(2,1)S(1)} %reshape.191), channel_id=1, source_target_pairs={{0,64},{64,128},{128,192},{192,256},{256,320},{320,384},{384,448},... | collective-permute-start | bytes 608264 | tf_op jit(solution)/shard_map/ppermute | solution.py:28
  36.7 4.2 %collective-permute-done.4 = bf16[3,264,128]{2,1,0:T(8,128)(2,1)S(1)} collective-permute-done((bf16[3,264,128]{2,1,0:T(8,128)(2,1)S(1)}, bf16[3,264,128]{2,1,0:T(8,128)(2,1)S(1)}, u32[]{:S(2)}, u32[]{:S(2)}) %collective-permute-start.4) | collective-permute-done | bytes 202784 | tf_op jit(solution)/shard_map/ppermute | solution.py:28
  40.9 3.8 %collective-permute-start.5 = (bf16[3,264,128]{2,1,0:T(8,128)(2,1)S(1)}, bf16[3,264,128]{2,1,0:T(8,128)(2,1)S(1)}, u32[]{:S(2)}, u32[]{:S(2)}) collective-permute-start(bf16[3,264,128]{2,1,0:T(8,128)(2,1)S(1)} %collective-permute-done.4), channel_id=1, source_target_pairs={{0,64},{64,128},{128,192},{192,256},{256,320},{320,384},{384,448},... | collective-permute-start | bytes 608264 | tf_op jit(solution)/shard_map/ppermute | solution.py:28
  48.5 5.0 %collective-permute-start.6 = (bf16[3,264,128]{2,1,0:T(8,128)(2,1)S(1)}, bf16[3,264,128]{2,1,0:T(8,128)(2,1)S(1)}, u32[]{:S(2)}, u32[]{:S(2)}) collective-permute-start(bf16[3,264,128]{2,1,0:T(8,128)(2,1)S(1)} %collective-permute-done.5), channel_id=1, source_target_pairs={{0,64},{64,128},{128,192},{192,256},{256,320},{320,384},{384,448},... | collective-permute-start | bytes 608264 | tf_op jit(solution)/shard_map/ppermute | solution.py:28
  56.8 5.6 %collective-permute-start.7 = (bf16[3,264,128]{2,1,0:T(8,128)(2,1)S(1)}, bf16[3,264,128]{2,1,0:T(8,128)(2,1)S(1)}, u32[]{:S(2)}, u32[]{:S(2)}) collective-permute-start(bf16[3,264,128]{2,1,0:T(8,128)(2,1)S(1)} %collective-permute-done.6), channel_id=1, source_target_pairs={{0,64},{64,128},{128,192},{192,256},{256,320},{320,384},{384,448},... | collective-permute-start | bytes 608264 | tf_op jit(solution)/shard_map/ppermute | solution.py:28
  65.8 5.9 %collective-permute-done.10 = bf16[3,264,128]{2,1,0:T(8,128)(2,1)S(1)} collective-permute-done((bf16[3,264,128]{2,1,0:T(8,128)(2,1)S(1)}, bf16[3,264,128]{2,1,0:T(8,128)(2,1)S(1)}, u32[]{:S(2)}, u32[]{:S(2)}) %collective-permute-start.10) | collective-permute-done | bytes 202784 | tf_op jit(solution)/shard_map/ppermute | solution.py:31
  79.1 2.5 %concatenate.35 = bf16[3,64,33,128]{3,2,1,0:T(8,128)(2,1)S(1)} reshape(bf16[3,8,264,128]{3,2,1,0:T(8,128)(2,1)} %copy.44) | data formatting | bytes 3244032 | tf_op jit(solution)/shard_map/concatenate | solution.py:53
  81.6 3.7 %concatenate.36 = bf16[3,64,33,128]{3,2,1,0:T(8,128)(2,1)} reshape(bf16[3,2112,128]{2,1,0:T(8,128)(2,1)} %collective-permute-done.11) | data formatting | bytes 3244032 | tf_op jit(solution)/shard_map/concatenate | solution.py:53
  85.2 2.9 %maximum_select_fusion = bf16[3,64,33,256]{3,2,1,0:T(8,128)(2,1)S(1)} fusion(bf16[3,64,33,128]{3,2,1,0:T(8,128)(2,1)} %concatenate.36, bf16[3,64,33,128]{3,2,1,0:T(8,128)(2,1)S(1)} %concatenate.35, pred[]{:T(512)S(6)} %eq.87), kind=kLoop, calls=%fused_computation.2 | loop fusion | flops 14598144 | bytes 6488065 | tf_op jit(solution)/shard_map/jit(_where)/select_n | solution.py:52
  90.2 31.1 %all-to-all-done = bf16[8,1024,256]{2,1,0:T(8,128)(2,1)} async-done(((bf16[8,1024,256]{2,1,0:T(8,128)(2,1)}), bf16[8,1024,256]{2,1,0:T(8,128)(2,1)}, u32[]{:S(2)}, u32[]{:S(2)}) %all-to-all-start) | async-done | bytes 4194336 | tf_op jit(solution)/shard_map/all_to_all | solution.py:15
  121.3 6.5 %copy.46 = bf16[1024,8,256]{2,1,0:T(8,128)(2,1)} copy(bf16[1024,8,256]{2,0,1:T(8,128)(2,1)} %bitcast.16) | data formatting | bytes 8388608 | tf_op jit(solution)/shard_map/reshape | solution.py:16
  127.9 7.4 %reshape.208 = bf16[1024,2048,1]{1,0,2:T(8,128)(2,1)} reshape(bf16[1024,8,256]{2,1,0:T(8,128)(2,1)} %copy.46) | data formatting | bytes 8388608 | tf_op jit(solution)/shard_map/reshape | solution.py:16
  135.3 4.6 %fusion.2 = bf16[2,1024,256]{1,2,0:T(8,128)(2,1)S(1)} fusion(bf16[2,2048,256]{2,1,0:T(8,128)(2,1)S(1)} %bitcast.95, bf16[1024,2048,1]{1,0,2:T(8,128)(2,1)} %reshape.208), kind=kOutput, calls=%fused_computation.18 | convolution fusion | flops 2148007936 | bytes 7340032 | tf_op jit(solution)/shard_map/tr,grc->gtc/dot_general | solution.py:121
  140.9 4.8 %copy.64 = bf16[8,128,8,256]{3,2,0,1:T(8,128)(2,1)} copy(bf16[8,128,8,256]{3,2,1,0:T(8,128)(2,1)} %bitcast.39) | data formatting | bytes 8388608 | tf_op jit(solution)/shard_map/reshape | solution.py:16
  147.1 4.8 %all-to-all-start.1 = ((bf16[8,2,128,128]{3,2,1,0:T(8,128)(2,1)}), bf16[8,2,128,128]{3,2,1,0:T(8,128)(2,1)S(1)}, u32[]{:S(2)}, u32[]{:S(2)}) async-start(bf16[8,2,128,128]{3,2,1,0:T(8,128)(2,1)} %broadcast_in_dim.115), calls=%async_computation.1 | async-start | bytes 1048576 | tf_op jit(solution)/shard_map/all_to_all | solution.py:91
  154.5 4.2 %fusion.14 = bf16[1024,256]{0,1:T(8,128)(2,1)S(1)} fusion(bf16[2048,256]{1,0:T(8,128)(2,1)} %bitcast.99, bf16[1024,2048]{1,0:T(8,128)(2,1)} %bitcast.93), kind=kOutput, calls=%fused_computation.32 | convolution fusion | flops 1075314688 | bytes 5767168 | tf_op jit(solution)/shard_map/tr,rc->tc/dot_general | solution.py:133
  162.3 2.9 %fusion.7 = f32[512,2,128]{0,2,1:T(8,128)S(1)} fusion(bf16[1024,2,128]{0,2,1:T(8,128)(2,1)} %bitcast.101, bf16[512,2,128]{0,2,1:T(8,128)(2,1)} %bitcast.104, pred[512,1024]{1,0:T(8,128)(4,1)} %fusion, f32[1024,2,128]{0,2,1:T(8,128)S(1)} %bitcast.98), kind=kOutput, calls=%fused_computation.25 | convolution fusion | flops 540278784 | bytes 2883584 | tf_op jit(solution)/shard_map/hbs,she->bhe/dot_general | solution.py:152
  165.5 5.7 %collective-permute-start.13 = (bf16[2,128,128]{2,1,0:T(8,128)(2,1)S(1)}, bf16[2,128,128]{2,1,0:T(8,128)(2,1)S(1)}, u32[]{:S(2)}, u32[]{:S(2)}) collective-permute-start(bf16[2,128,128]{2,1,0:T(8,128)(2,1)S(1)} %get-tuple-element.10), channel_id=1, source_target_pairs={{0,128},{64,192},{128,256},{192,320},{256,384},{320,448},{1,129},{... | collective-permute-start | bytes 196616 | tf_op jit(solution)/shard_map/ppermute | solution.py:20
  171.2 2.6 %collective-permute-start.12 = (bf16[2,128,128]{2,1,0:T(8,128)(2,1)S(1)}, bf16[2,128,128]{2,1,0:T(8,128)(2,1)S(1)}, u32[]{:S(2)}, u32[]{:S(2)}) collective-permute-start(bf16[2,128,128]{2,1,0:T(8,128)(2,1)S(1)} %get-tuple-element.9), channel_id=1, source_target_pairs={{0,64},{64,128},{128,192},{192,256},{256,320},{320,384},{384,448},... | collective-permute-start | bytes 196616 | tf_op jit(solution)/shard_map/ppermute | solution.py:20
  175.1 2.3 %collective-permute-done.12 = bf16[2,128,128]{2,1,0:T(8,128)(2,1)S(1)} collective-permute-done((bf16[2,128,128]{2,1,0:T(8,128)(2,1)S(1)}, bf16[2,128,128]{2,1,0:T(8,128)(2,1)S(1)}, u32[]{:S(2)}, u32[]{:S(2)}) %collective-permute-start.12) | collective-permute-done | bytes 65568 | tf_op jit(solution)/shard_map/ppermute | solution.py:20
  (88 shorter events, 40.9 us)
Async XLA Ops:
  2.8 3.1 %collective-permute-start = (bf16[3,33,256]{2,1,0:T(8,128)(2,1)S(1)}, bf16[3,33,256]{2,1,0:T(8,128)(2,1)S(1)}, u32[]{:S(2)}, u32[]{:S(2)}) collective-permute-start(bf16[3,33,256]{2,1,0:T(8,128)(2,1)S(1)} %concatenate.31), channel_id=1, source_target_pairs={{0,8},{8,0},{1,9},{9,1},{2,10},{10,2},{3,11},{11,3},{4,12},{12,4},... | collective-permute-start | bytes 152072 | tf_op jit(solution)/shard_map/ppermute | solution.py:45
  7.4 23.5 %collective-permute-start.1 = (bf16[3,66,128]{2,1,0:T(8,128)(2,1)S(1)}, bf16[3,66,128]{2,1,0:T(8,128)(2,1)S(1)}, u32[]{:S(2)}, u32[]{:S(2)}) collective-permute-start(bf16[3,66,128]{2,1,0:T(8,128)(2,1)S(1)} %pad_maximum_fusion), channel_id=1, source_target_pairs={{0,32},{16,48},{32,0},{48,16},{1,33},{17,49},{33,1},{49,17},{2,34}... | collective-permute-start | bytes 152072 | tf_op jit(solution)/shard_map/ppermute | solution.py:62
  14.7 106.6 %all-to-all-start = ((bf16[8,1024,256]{2,1,0:T(8,128)(2,1)}), bf16[8,1024,256]{2,1,0:T(8,128)(2,1)}, u32[]{:S(2)}, u32[]{:S(2)}) async-start(bf16[8,1024,256]{2,1,0:T(8,128)(2,1)} %stack.57), calls=%async_computation | async-start | bytes 8388608 | tf_op jit(solution)/shard_map/all_to_all | solution.py:15
  25.0 6.0 %collective-permute-start.2 = (bf16[3,66,128]{2,1,0:T(8,128)(2,1)S(1)}, bf16[3,66,128]{2,1,0:T(8,128)(2,1)S(1)}, u32[]{:S(2)}, u32[]{:S(2)}) collective-permute-start(bf16[3,66,128]{2,1,0:T(8,128)(2,1)S(1)} %pad_maximum_fusion), channel_id=1, source_target_pairs={{0,16},{16,32},{32,48},{48,0},{1,17},{17,33},{33,49},{49,1},{2,18}... | collective-permute-start | bytes 152072 | tf_op jit(solution)/shard_map/ppermute | solution.py:62
  27.0 6.0 %collective-permute-start.3 = (bf16[3,66,128]{2,1,0:T(8,128)(2,1)S(1)}, bf16[3,66,128]{2,1,0:T(8,128)(2,1)S(1)}, u32[]{:S(2)}, u32[]{:S(2)}) collective-permute-start(bf16[3,66,128]{2,1,0:T(8,128)(2,1)S(1)} %pad_maximum_fusion), channel_id=1, source_target_pairs={{0,48},{16,0},{32,16},{48,32},{1,49},{17,1},{33,17},{49,33},{2,50}... | collective-permute-start | bytes 152072 | tf_op jit(solution)/shard_map/ppermute | solution.py:62
  33.2 7.7 %collective-permute-start.4 = (bf16[3,264,128]{2,1,0:T(8,128)(2,1)S(1)}, bf16[3,264,128]{2,1,0:T(8,128)(2,1)S(1)}, u32[]{:S(2)}, u32[]{:S(2)}) collective-permute-start(bf16[3,264,128]{2,1,0:T(8,128)(2,1)S(1)} %reshape.191), channel_id=1, source_target_pairs={{0,64},{64,128},{128,192},{192,256},{256,320},{320,384},{384,448},... | collective-permute-start | bytes 608264 | tf_op jit(solution)/shard_map/ppermute | solution.py:28
  40.9 7.6 %collective-permute-start.5 = (bf16[3,264,128]{2,1,0:T(8,128)(2,1)S(1)}, bf16[3,264,128]{2,1,0:T(8,128)(2,1)S(1)}, u32[]{:S(2)}, u32[]{:S(2)}) collective-permute-start(bf16[3,264,128]{2,1,0:T(8,128)(2,1)S(1)} %collective-permute-done.4), channel_id=1, source_target_pairs={{0,64},{64,128},{128,192},{192,256},{256,320},{320,384},{384,448},... | collective-permute-start | bytes 608264 | tf_op jit(solution)/shard_map/ppermute | solution.py:28
  44.7 9.3 %collective-permute-start.8 = (bf16[3,264,128]{2,1,0:T(8,128)(2,1)S(1)}, bf16[3,264,128]{2,1,0:T(8,128)(2,1)S(1)}, u32[]{:S(2)}, u32[]{:S(2)}) collective-permute-start(bf16[3,264,128]{2,1,0:T(8,128)(2,1)S(1)} %reshape.191), channel_id=1, source_target_pairs={{0,448},{64,0},{128,64},{192,128},{256,192},{320,256},{384,320},{4... | collective-permute-start | bytes 608264 | tf_op jit(solution)/shard_map/ppermute | solution.py:31
  48.5 8.2 %collective-permute-start.6 = (bf16[3,264,128]{2,1,0:T(8,128)(2,1)S(1)}, bf16[3,264,128]{2,1,0:T(8,128)(2,1)S(1)}, u32[]{:S(2)}, u32[]{:S(2)}) collective-permute-start(bf16[3,264,128]{2,1,0:T(8,128)(2,1)S(1)} %collective-permute-done.5), channel_id=1, source_target_pairs={{0,64},{64,128},{128,192},{192,256},{256,320},{320,384},{384,448},... | collective-permute-start | bytes 608264 | tf_op jit(solution)/shard_map/ppermute | solution.py:28
  54.0 8.8 %collective-permute-start.9 = (bf16[3,264,128]{2,1,0:T(8,128)(2,1)S(1)}, bf16[3,264,128]{2,1,0:T(8,128)(2,1)S(1)}, u32[]{:S(2)}, u32[]{:S(2)}) collective-permute-start(bf16[3,264,128]{2,1,0:T(8,128)(2,1)S(1)} %collective-permute-done.8), channel_id=1, source_target_pairs={{0,448},{64,0},{128,64},{192,128},{256,192},{320,256},{384,320},{4... | collective-permute-start | bytes 608264 | tf_op jit(solution)/shard_map/ppermute | solution.py:31
  56.8 8.8 %collective-permute-start.7 = (bf16[3,264,128]{2,1,0:T(8,128)(2,1)S(1)}, bf16[3,264,128]{2,1,0:T(8,128)(2,1)S(1)}, u32[]{:S(2)}, u32[]{:S(2)}) collective-permute-start(bf16[3,264,128]{2,1,0:T(8,128)(2,1)S(1)} %collective-permute-done.6), channel_id=1, source_target_pairs={{0,64},{64,128},{128,192},{192,256},{256,320},{320,384},{384,448},... | collective-permute-start | bytes 608264 | tf_op jit(solution)/shard_map/ppermute | solution.py:28
  62.8 8.9 %collective-permute-start.10 = (bf16[3,264,128]{2,1,0:T(8,128)(2,1)S(1)}, bf16[3,264,128]{2,1,0:T(8,128)(2,1)S(1)}, u32[]{:S(2)}, u32[]{:S(2)}) collective-permute-start(bf16[3,264,128]{2,1,0:T(8,128)(2,1)S(1)} %collective-permute-done.9), channel_id=1, source_target_pairs={{0,448},{64,0},{128,64},{192,128},{256,192},{320,256},{384,320},{4... | collective-permute-start | bytes 608264 | tf_op jit(solution)/shard_map/ppermute | solution.py:31
  72.1 4.1 %copy-start.1 = (s32[1024]{0:T(1024)S(1)}, s32[1024]{0:T(1024)}, u32[]{:S(2)}) copy-start(s32[1024]{0:T(1024)} %param.7) | copy-start | bytes 12292
  73.6 7.9 %collective-permute-start.11 = (bf16[3,2112,128]{2,1,0:T(8,128)(2,1)}, bf16[3,2112,128]{2,1,0:T(8,128)(2,1)}, u32[]{:S(2)}, u32[]{:S(2)}) collective-permute-start(bf16[3,2112,128]{2,1,0:T(8,128)(2,1)} %bitcast.14), channel_id=1, source_target_pairs={{0,8},{8,0},{1,9},{9,1},{2,10},{10,2},{3,11},{11,3},{4,12},{12,4},... | collective-permute-start | bytes 4866056 | tf_op jit(solution)/shard_map/ppermute | solution.py:51
  140.1 5.5 %copy-start = (bf16[1,1024,256]{1,2,0:T(8,128)(2,1)}, bf16[1,1024,256]{1,2,0:T(8,128)(2,1)S(1)}, u32[]{:S(2)}) copy-start(bf16[1,1024,256]{1,2,0:T(8,128)(2,1)S(1)} %get-tuple-element.17) | copy-start | bytes 1572868
  147.1 18.0 %all-to-all-start.1 = ((bf16[8,2,128,128]{3,2,1,0:T(8,128)(2,1)}), bf16[8,2,128,128]{3,2,1,0:T(8,128)(2,1)S(1)}, u32[]{:S(2)}, u32[]{:S(2)}) async-start(bf16[8,2,128,128]{3,2,1,0:T(8,128)(2,1)} %broadcast_in_dim.115), calls=%async_computation.1 | async-start | bytes 1048576 | tf_op jit(solution)/shard_map/all_to_all | solution.py:91
  165.1 12.6 %copy-start.2 = (f32[256]{0:T(256)S(1)}, f32[256]{0:T(256)}, u32[]{:S(2)}) copy-start(f32[256]{0:T(256)} %param.6) | copy-start | bytes 3076
  165.5 9.6 %collective-permute-start.13 = (bf16[2,128,128]{2,1,0:T(8,128)(2,1)S(1)}, bf16[2,128,128]{2,1,0:T(8,128)(2,1)S(1)}, u32[]{:S(2)}, u32[]{:S(2)}) collective-permute-start(bf16[2,128,128]{2,1,0:T(8,128)(2,1)S(1)} %get-tuple-element.10), channel_id=1, source_target_pairs={{0,128},{64,192},{128,256},{192,320},{256,384},{320,448},{1,129},{... | collective-permute-start | bytes 196616 | tf_op jit(solution)/shard_map/ppermute | solution.py:20
  171.2 6.2 %collective-permute-start.12 = (bf16[2,128,128]{2,1,0:T(8,128)(2,1)S(1)}, bf16[2,128,128]{2,1,0:T(8,128)(2,1)S(1)}, u32[]{:S(2)}, u32[]{:S(2)}) collective-permute-start(bf16[2,128,128]{2,1,0:T(8,128)(2,1)S(1)} %get-tuple-element.9), channel_id=1, source_target_pairs={{0,64},{64,128},{128,192},{192,256},{256,320},{320,384},{384,448},... | collective-permute-start | bytes 196616 | tf_op jit(solution)/shard_map/ppermute | solution.py:20
